TPU v7x, 32 devices: a whole 2x2x4 slice. The times are simulated.
32 devices in a mesh: groups: 2 (over y), gx: 4 (over z), gy: 2 (over x), gz: 2 (over core).
Axes of the slice: x: 2, y: 2, z: 4, core: 2. Of those that a mesh axis runs over, the one named last changes fastest.
Arguments:
- parent: bfloat16 [160, 32, 1024], P('groups', 'gx', ('gy', 'gz')), parts along dimension 0, may hold values from -6 to 6
- nest: bfloat16 [160, 24, 1536], P('groups', 'gx', ('gy', 'gz')), parts along dimension 0, may hold values from -6 to 6
- nu_parent: float32 [80], replicated, may hold values from 0.03 to 0.24
- nu_nest: float32 [80], replicated, may hold values from 0.03 to 0.24
- relax: float32 [80], replicated, may hold values from 0.1 to 0.5
- feedback: float32 [80], replicated, may hold values from 0.3 to 1
- vert_mix: float32 [80, 80], replicated, may hold values from -1 to 1
- fp_owner: int32 [4, 4, 256, 1], P('gx', ('gy', 'gz')), may hold values from 0 to 3; in each aligned block of 256 rows (0 to 255, 256 to 511, ..., all dimensions but the last counted through in order) at most 256 rows name the same one
- fp_cell: int32 [4, 4, 256], P('gx', ('gy', 'gz')), may hold values from 0 to 2047
- nest_of: int32 [24], replicated, may hold values from 0 to 2, as said below
Outputs:
- parent_out: bfloat16 [160, 32, 1024], P('groups', 'gx', ('gy', 'gz')), parts along dimension 0
- nest_out: bfloat16 [160, 24, 1536], P('groups', 'gx', ('gy', 'gz')), parts along dimension 0
There are 2 independent parts, one for each index of `groups`. A program takes and returns all parts, laid end to end along the dimension named above; an argument that names none is the same for every part. Nothing has to cross between parts.
Inputs may be any that keep to these rules, and one draw needn't show every extreme that they name: `fp_owner`: within the 256 blocks of one nest tile no parent tile is named more than 256 times; in some nest tiles one is named exactly 256 times. `nest_of`: never falls along the rows; every nest holds one or more rows; nest 1 holds rows 11 and 12.
All inputs are finite; a program needn't handle non-finite values.
Results may differ from a plain program's by a relative error of at most 0.0033.
Values may be sent and summed in bfloat16 or wider, within the bound.
No kernel may reach another device: no remote copies, remote signals or barrier semaphores. Data moves between devices by JAX's collectives and lax.ppermute only.
A program may use at most 64 MiB of HBM per device.

v0:
```python
import jax
import jax.numpy as jnp
from jax import lax
from jax.sharding import PartitionSpec as P

Y_AXES = ("gy", "gz")
HI = lax.Precision.HIGHEST


def shift_pairs(count):
    forward = [(i, i + 1) for i in range(count - 1)]
    backward = [(i + 1, i) for i in range(count - 1)]
    return (forward, backward)


def exchange(blocks):
    fwd_x, bwd_x = shift_pairs(lax.axis_size("gx"))
    fwd_y, bwd_y = shift_pairs(lax.axis_size(Y_AXES))
    last_rows = jnp.concatenate([b[:, -1, :] for b in blocks], axis=1)
    first_rows = jnp.concatenate([b[:, 0, :] for b in blocks], axis=1)
    last_cols = jnp.concatenate([b[:, :, -1] for b in blocks], axis=1)
    first_cols = jnp.concatenate([b[:, :, 0] for b in blocks], axis=1)
    above = lax.ppermute(last_rows, "gx", fwd_x)
    below = lax.ppermute(first_rows, "gx", bwd_x)
    left = lax.ppermute(last_cols, Y_AXES, fwd_y)
    right = lax.ppermute(first_cols, Y_AXES, bwd_y)
    out = []
    xo = 0
    yo = 0
    for b in blocks:
        w, h = (b.shape[2], b.shape[1])
        out.append(
            (
                above[:, xo : xo + w],
                below[:, xo : xo + w],
                left[:, yo : yo + h],
                right[:, yo : yo + h],
            )
        )
        xo += w
        yo += h
    return out


def per_row(values, rows, cols):
    if values.ndim == 1:
        return jnp.broadcast_to(values[:, None], (rows, cols)).reshape(rows * cols)
    return jnp.broadcast_to(values[:, :, None], values.shape + (cols,)).reshape(
        values.shape[0], rows * cols
    )


def flat_stencil(flat, rows, cols, halo, up_w=None, down_w=None):
    above, below, left, right = (h.astype(flat.dtype) for h in halo)
    levels = flat.shape[0]
    up = jnp.concatenate([above, flat[:, :-cols]], axis=1)
    down = jnp.concatenate([flat[:, cols:], below], axis=1)
    col = lax.broadcasted_iota(jnp.int32, (1, rows * cols), 1) % cols
    zero = jnp.zeros((levels, 1), flat.dtype)
    west = jnp.where(
        col == 0, per_row(left, rows, cols), jnp.concatenate([zero, flat[:, :-1]], axis=1)
    )
    east = jnp.where(
        col == cols - 1, per_row(right, rows, cols), jnp.concatenate([flat[:, 1:], zero], axis=1)
    )
    if down_w is not None:
        down = down * down_w[None, :]
        up = up * up_w[None, :]
    return down + up + east + west - 4.0 * flat


def mix_levels(matrix, flat):
    return jnp.dot(matrix, flat, precision=HI, preferred_element_type=jnp.float32)


def nest_segments(nest_of, first, count):
    index_rows = first + jnp.arange(count, dtype=jnp.int32)
    inside = (index_rows >= 0) & (index_rows < nest_of.shape[0])
    return jnp.where(inside, nest_of[jnp.clip(index_rows, 0, nest_of.shape[0] - 1)], -1)


def row_weights(segments):
    left_w = (segments[:-2] == segments[1:-1]).astype(jnp.float32)
    right_w = (segments[2:] == segments[1:-1]).astype(jnp.float32)
    return (left_w, right_w)


def block_expansion(block_rows, block_cols, rows, cols, zero):
    r = lax.broadcasted_iota(jnp.int32, (block_rows * block_cols, rows * cols), 0) + zero
    p = lax.broadcasted_iota(jnp.int32, (block_rows * block_cols, rows * cols), 1)
    hit = (p // cols // 3 == r // block_cols) & (p % cols // 3 == r % block_cols)
    return hit.astype(jnp.float32)


def body(parent, nest, nu_parent, nu_nest, relax, feedback, vert_mix, fp_owner, fp_cell, nest_of):
    levels, p_rows, p_cols = parent.shape
    _, n_rows, n_cols = nest.shape
    tiles_x = lax.axis_size("gx")
    here_x = lax.axis_index("gx")
    zero = jnp.minimum(here_x, 0)
    parent_halo, nest_halo = exchange([parent, nest])
    centre = parent.astype(jnp.float32).reshape(levels, p_rows * p_cols)
    stencil = flat_stencil(centre, p_rows, p_cols, parent_halo)
    flat_parent = mix_levels(vert_mix, centre + nu_parent[:, None] * stencil)
    owners = fp_owner.reshape(-1)
    cells = fp_cell.reshape(-1)
    requests = owners.shape[0]
    slots = 4 * requests // tiles_x
    owner_ids = jnp.arange(tiles_x, dtype=jnp.int32)
    if slots >= requests:
        chosen = owners[None, :] == owner_ids[:, None]
        wanted = jnp.where(chosen, cells[None, :], 0)
        wanted = jnp.pad(wanted, ((0, 0), (0, slots - requests))).reshape(-1)
    else:
        onehot = (owners[:, None] == owner_ids[None, :]).astype(jnp.int32)
        before = jnp.cumsum(onehot, axis=0) - onehot
        order_in = jnp.sum(before * onehot, axis=1)
        places = owners * slots + order_in
        wanted = jnp.zeros((tiles_x * slots,), jnp.int32).at[places].set(cells)
    served_ids = lax.all_to_all(wanted, "gx", split_axis=0, concat_axis=0, tiled=True)
    answers = lax.all_to_all(
        jnp.take(flat_parent, served_ids, axis=1), "gx", split_axis=1, concat_axis=1, tiled=True
    )
    if slots >= requests:
        answers = answers.reshape(levels, tiles_x, slots)[:, :, :requests]
        forcing_flat = answers[:, 0, :]
        for o in range(1, tiles_x):
            forcing_flat = jnp.where(chosen[o][None, :], answers[:, o, :], forcing_flat)
    else:
        forcing_flat = jnp.take(answers, places, axis=1)
    block_rows = n_rows // 3
    block_cols = n_cols // 3
    expand = block_expansion(block_rows, block_cols, n_rows, n_cols, zero)
    forcing_full = jnp.dot(forcing_flat, expand, precision=HI, preferred_element_type=jnp.float32)
    row_start = here_x * n_rows
    left_w, right_w = row_weights(nest_segments(nest_of, row_start - 1, n_rows + 2))
    up_w = per_row(left_w, n_rows, n_cols)
    down_w = per_row(right_w, n_rows, n_cols)
    nest_state = nest.astype(jnp.float32).reshape(levels, n_rows * n_cols)
    halo = nest_halo
    for turn_no in range(3):
        if turn_no > 0:
            shaped = nest_state.astype(jnp.bfloat16).reshape(levels, n_rows, n_cols)
            (halo,) = exchange([shaped])
        stencil_sum = flat_stencil(nest_state, n_rows, n_cols, halo, up_w, down_w)
        moved = nest_state + nu_nest[:, None] * stencil_sum
        moved = moved + relax[:, None] * (forcing_full - moved)
        nest_state = mix_levels(vert_mix, moved)
    block_sum = lax.dot_general(
        nest_state,
        expand,
        (((1,), (1,)), ((), ())),
        precision=HI,
        preferred_element_type=jnp.float32,
    )
    nudge_gap = block_sum / 9.0 - forcing_flat
    if slots >= requests:
        outgoing = jnp.where(chosen[None, :, :], nudge_gap[:, None, :], 0.0)
        outgoing = jnp.pad(outgoing, ((0, 0), (0, 0), (0, slots - requests)))
        outgoing = outgoing.reshape(levels, tiles_x * slots)
    else:
        outgoing = jnp.zeros((levels, tiles_x * slots), jnp.float32).at[:, places].set(nudge_gap)
    incoming = lax.all_to_all(outgoing, "gx", split_axis=1, concat_axis=1, tiled=True)
    summed = jnp.zeros_like(flat_parent).at[:, served_ids].add(incoming)
    parent_out = (flat_parent + feedback[:, None] * summed).astype(jnp.bfloat16)
    return (
        parent_out.reshape(levels, p_rows, p_cols),
        nest_state.astype(jnp.bfloat16).reshape(levels, n_rows, n_cols),
    )


def solution(mesh):
    placed = (
        P("groups", "gx", Y_AXES),
        P("groups", "gx", Y_AXES),
        P(),
        P(),
        P(),
        P(),
        P(),
        P("gx", Y_AXES, None, None),
        P("gx", Y_AXES, None),
        P(),
    )
    return jax.shard_map(
        body,
        mesh=mesh,
        in_specs=placed,
        out_specs=(P("groups", "gx", Y_AXES), P("groups", "gx", Y_AXES)),
        check_vma=False,
    )
```

profile of v0, /device:TPU:1, one launch (start us, length us, event | category | flops | bytes accessed | tf_op | source)
XLA Modules:
  0.0 121.2 jit_solution(3893287503478127455)
XLA Ops:
  0.7 0.9 slice_bitcast_fusion.4
  1.6 1.2 %fusion.144 = (bf16[80,1,256]{2,1,0:T(2,128)(2,1)S(1)}, bf16[80,1,256]{2,1,0:T(2,128)(2,1)S(1)}) fusion(bf16[80,8,256]{2,1,0:T(8,128)(2,1)} %param.10), kind=kLoop, calls=%fused_computation.220 | loop fusion | bytes 163840 | tf_op jit(solution)/shard_map/slice | solution.py:19
  2.8 0.7 pad_maximum_fusion
  3.5 1.4 %collective-permute-start = (bf16[80,640]{1,0:T(8,128)(2,1)}, bf16[80,640]{1,0:T(8,128)(2,1)}, u32[]{:S(2)}, u32[]{:S(2)}) collective-permute-start(bf16[80,640]{1,0:T(8,128)(2,1)} %pad_maximum_fusion), channel_id=1, source_target_pairs={{4,0},{8,4},{12,8},{5,1},{9,5},{13,9},{6,2},{10,6},{14,10},{7,3},{... | collective-permute-start | bytes 307208 | tf_op jit(solution)/shard_map/ppermute | solution.py:24
  4.9 0.7 pad_maximum_fusion.1
  5.6 5.3 %collective-permute-start.1 = (bf16[80,640]{1,0:T(8,128)(2,1)}, bf16[80,640]{1,0:T(8,128)(2,1)}, u32[]{:S(2)}, u32[]{:S(2)}) collective-permute-start(bf16[80,640]{1,0:T(8,128)(2,1)} %pad_maximum_fusion.1), channel_id=1, source_target_pairs={{0,4},{4,8},{8,12},{1,5},{5,9},{9,13},{2,6},{6,10},{10,14},{3,7},{... | collective-permute-start | bytes 307208 | tf_op jit(solution)/shard_map/ppermute | solution.py:23
  11.4 4.4 %collective-permute-start.3 = (bf16[80,14]{0,1:T(8,128)(2,1)S(1)}, bf16[80,14]{0,1:T(8,128)(2,1)S(1)}, u32[]{:S(2)}, u32[]{:S(2)}) collective-permute-start(bf16[80,14]{0,1:T(8,128)(2,1)S(1)} %pad_maximum_fusion.3), channel_id=1, source_target_pairs={{0,1},{1,2},{2,3},{4,5},{5,6},{6,7},{8,9},{9,10},{10,11},{12,13},{... | collective-permute-start | bytes 6728 | tf_op jit(solution)/shard_map/ppermute | solution.py:25
  16.1 1.9 %collective-permute-start.2 = (bf16[80,14]{0,1:T(8,128)(2,1)S(1)}, bf16[80,14]{0,1:T(8,128)(2,1)S(1)}, u32[]{:S(2)}, u32[]{:S(2)}) collective-permute-start(bf16[80,14]{0,1:T(8,128)(2,1)S(1)} %pad_maximum_fusion.2), channel_id=1, source_target_pairs={{1,0},{2,1},{3,2},{5,4},{6,5},{7,6},{9,8},{10,9},{11,10},{13,12},{... | collective-permute-start | bytes 6728 | tf_op jit(solution)/shard_map/ppermute | solution.py:26
  18.1 0.6 compare_select_fusion.1
  18.7 3.6 %all-to-all-start = ((s32[4,256,1]{1,2,0:T(1,128)}), s32[4,256,1]{1,2,0:T(1,128)S(1)}, u32[]{:S(2)}, u32[]{:S(2)}) async-start(s32[4,256,1]{1,2,0:T(1,128)} %compare_select_fusion.1), calls=%async_computation | async-start | bytes 8192 | tf_op jit(solution)/shard_map/all_to_all | solution.py:120
  22.3 1.1 fusion.137
  23.9 1.1 fusion.135
  25.0 1.4 %fusion.134 = (f32[80,2303]{1,0:T(8,128)}, f32[80,2303]{1,0:T(8,128)}) fusion(f32[80,2304]{1,0:T(8,128)S(1)} %bitcast.111), kind=kLoop, calls=%fused_computation.210 | loop fusion | bytes 2947840 | tf_op jit(solution)/shard_map/slice | solution.py:64
  26.4 0.6 gather_fusion
  27.2 2.2 %fusion.6 = pred[256,2304]{1,0:T(32,128)(4,1)} fusion(s32[256]{0:T(256)S(1)} %get-tuple-element.58, s32[256]{0:T(256)S(1)} %get-tuple-element.59, s32[2304]{0:T(1024)S(1)} %get-tuple-element.62, s32[2304]{0:T(1024)S(1)} %get-tuple-element.63, s32[256]{0:T(256)S(1)} %get-tuple-element.57, s32[256]{0:T(256)S(1)} %get-tuple-element.60, ...), kind=kLoop, calls=%fused_computation.20 | loop fusion | flops 13565952 | bytes 635904 | tf_op jit(solution)/shard_map/and | solution.py:91
  29.8 1.0 copy.130
  31.1 1.0 copy.129
  32.2 0.8 slice_convert_fusion.3
  33.0 0.8 slice_convert_fusion.2
  33.8 2.8 %convolution_bitcast_fusion.2 = f32[80,2048]{1,0:T(8,128)S(1)} fusion(f32[80,80]{1,0:T(8,128)S(1)} %copy-done, f32[80,2048]{1,0:T(8,128)S(1)} %bitcast.115, f32[80,256]{1,0:T(8,128)S(1)} %slice_convert_fusion.3, f32[80,1792]{1,0:T(8,128)} %get-tuple-element.28, f32[80,1792]{1,0:T(8,128)} %get-tuple-element.27, f32[80,256]{1,0:T(8,128)S(1)} %slice_convert_fusion.2, ...), kind=kOutput, calls=%fused_computation.13 | convolution fusion | flops 159088640 | bytes 5272256 | tf_op jit(solution)/shard_map/dot_general | solution.py:73
  36.6 0.3 copy.93
  36.9 2.8 %gather_fusion.1 = f32[1024,80]{1,0:T(8,128)S(1)} fusion(f32[80,2048]{0,1:T(8,128)S(1)} %copy.93, s32[1024]{0:T(1024)S(1)} %broadcast_clamp_fusion), kind=kCustom, calls=%fused_computation.1 | custom fusion | bytes 659456 | tf_op jit(solution)/shard_map/jit(_take)/gather | solution.py:122
  39.9 0.8 broadcast_select_fusion.1
  40.7 4.5 %all-to-all-start.1 = ((f32[80,4,256]{2,0,1:T(8,128)}), f32[80,4,256]{2,0,1:T(8,128)S(1)}, u32[]{:S(2)}, u32[]{:S(2)}) async-start(f32[80,4,256]{2,0,1:T(8,128)} %broadcast_select_fusion.1), calls=%async_computation.1 | async-start | bytes 655360 | tf_op jit(solution)/shard_map/all_to_all | solution.py:121
  45.5 1.0 copy.132
  46.8 1.0 copy.131
  47.8 1.5 %slice_convert_fusion = f32[80,384]{1,0:T(8,128)} fusion(bf16[80,640]{1,0:T(8,128)(2,1)} %collective-permute-done.1), kind=kLoop, calls=%fused_computation.131 | loop fusion | flops 30720 | bytes 184320 | tf_op jit(solution)/shard_map/convert_element_type | solution.py:54
  49.3 1.6 %slice_convert_fusion.1 = f32[80,384]{1,0:T(8,128)} fusion(bf16[80,640]{1,0:T(8,128)(2,1)} %collective-permute-done), kind=kLoop, calls=%fused_computation.132 | loop fusion | flops 30720 | bytes 184320 | tf_op jit(solution)/shard_map/convert_element_type | solution.py:54
  50.8 3.9 %all-to-all-done.1 = f32[80,4,256]{2,0,1:T(8,128)S(1)} async-done(((f32[80,4,256]{2,0,1:T(8,128)}), f32[80,4,256]{2,0,1:T(8,128)S(1)}, u32[]{:S(2)}, u32[]{:S(2)}) %all-to-all-start.1) | async-done | bytes 327712 | tf_op jit(solution)/shard_map/all_to_all | solution.py:121
  54.8 0.8 fusion.148
  55.7 3.3 %fusion.145 = (bf16[80,2304]{1,0:T(8,128)(2,1)S(1)}, f32[80,2304]{1,0:T(8,128)S(1)}) fusion(f32[80,80]{1,0:T(8,128)S(1)} %copy-done, f32[80,2304]{1,0:T(8,128)S(1)} %fusion.148, f32[80,2304]{1,0:T(8,128)S(1)} %bitcast.112, f32[80,1920]{1,0:T(8,128)} %get-tuple-element.23, f32[80,384]{1,0:T(8,128)S(1)} %copy-done.16, f32[80,384]{1,0:T(8,128)S(1)} %copy-done.17, ...), kind=kOutput, calls=%fused_computation.221 | convolution fusion | flops 180080640 | bytes 7052800 | tf_op jit(solution)/shard_map/dot_general | solution.py:73
  59.0 0.4 reshape.289
  59.7 1.3 %collective-permute-start.5 = (bf16[80,384]{1,0:T(8,128)(2,1)S(1)}, bf16[80,384]{1,0:T(8,128)(2,1)S(1)}, u32[]{:S(2)}, u32[]{:S(2)}) collective-permute-start(bf16[80,384]{1,0:T(8,128)(2,1)S(1)} %bitcast.142), channel_id=1, source_target_pairs={{0,4},{4,8},{8,12},{1,5},{5,9},{9,13},{2,6},{6,10},{10,14},{3,7},{... | collective-permute-start | bytes 184328 | tf_op jit(solution)/shard_map/ppermute | solution.py:23
  61.1 1.3 %collective-permute-start.4 = (bf16[80,384]{1,0:T(8,128)(2,1)S(1)}, bf16[80,384]{1,0:T(8,128)(2,1)S(1)}, u32[]{:S(2)}, u32[]{:S(2)}) collective-permute-start(bf16[80,384]{1,0:T(8,128)(2,1)S(1)} %bitcast.144), channel_id=1, source_target_pairs={{4,0},{8,4},{12,8},{5,1},{9,5},{13,9},{6,2},{10,6},{14,10},{7,3},{... | collective-permute-start | bytes 184328 | tf_op jit(solution)/shard_map/ppermute | solution.py:24
  62.5 4.4 %collective-permute-start.7 = (bf16[80,6]{0,1:T(8,128)(2,1)S(1)}, bf16[80,6]{0,1:T(8,128)(2,1)S(1)}, u32[]{:S(2)}, u32[]{:S(2)}) collective-permute-start(bf16[80,6]{0,1:T(8,128)(2,1)S(1)} %bitcast.154), channel_id=1, source_target_pairs={{0,1},{1,2},{2,3},{4,5},{5,6},{6,7},{8,9},{9,10},{10,11},{12,13},{... | collective-permute-start | bytes 2888 | tf_op jit(solution)/shard_map/ppermute | solution.py:25
  66.9 1.1 fusion.132
  68.2 1.9 %collective-permute-start.6 = (bf16[80,6]{0,1:T(8,128)(2,1)S(1)}, bf16[80,6]{0,1:T(8,128)(2,1)S(1)}, u32[]{:S(2)}, u32[]{:S(2)}) collective-permute-start(bf16[80,6]{0,1:T(8,128)(2,1)S(1)} %bitcast.156), channel_id=1, source_target_pairs={{1,0},{2,1},{3,2},{5,4},{6,5},{7,6},{9,8},{10,9},{11,10},{13,12},{... | collective-permute-start | bytes 2888 | tf_op jit(solution)/shard_map/ppermute | solution.py:26
  70.1 1.1 fusion.133
  71.5 1.0 copy.134
  72.5 0.6 collective-permute-done.6
  73.6 0.7 copy-done.13
  74.3 0.3 copy-done.7
  74.9 1.3 %fusion.146 = (bf16[80,2304]{1,0:T(8,128)(2,1)S(1)}, f32[80,2304]{1,0:T(8,128)S(1)}) fusion(f32[80,80]{1,0:T(8,128)S(1)} %copy-done, f32[80,2304]{1,0:T(8,128)S(1)} %fusion.148, f32[80,2304]{1,0:T(8,128)S(1)} %get-tuple-element.48, f32[80,1920]{1,0:T(8,128)S(1)} %copy-done.12, f32[80,384]{1,0:T(8,128)S(1)} %convert_element_type.84, ...), kind=kOutput, calls=%fused_computation.222 | convolution fusion | flops 180080640 | bytes 7052800 | tf_op jit(solution)/shard_map/dot_general | solution.py:73
  76.3 0.4 reshape.292
  77.0 4.9 %collective-permute-start.9 = (bf16[80,384]{1,0:T(8,128)(2,1)S(1)}, bf16[80,384]{1,0:T(8,128)(2,1)}, u32[]{:S(2)}, u32[]{:S(2)}) collective-permute-start(bf16[80,384]{1,0:T(8,128)(2,1)S(1)} %bitcast.143), channel_id=1, source_target_pairs={{0,4},{4,8},{8,12},{1,5},{5,9},{9,13},{2,6},{6,10},{10,14},{3,7},{... | collective-permute-start | bytes 184328 | tf_op jit(solution)/shard_map/ppermute | solution.py:23
  81.9 0.6 copy.150
  82.5 1.5 %collective-permute-start.8 = (bf16[80,384]{1,0:T(8,128)(2,1)}, bf16[80,384]{1,0:T(8,128)(2,1)}, u32[]{:S(2)}, u32[]{:S(2)}) collective-permute-start(bf16[80,384]{1,0:T(8,128)(2,1)} %bitcast.105), channel_id=1, source_target_pairs={{4,0},{8,4},{12,8},{5,1},{9,5},{13,9},{6,2},{10,6},{14,10},{7,3},{... | collective-permute-start | bytes 184328 | tf_op jit(solution)/shard_map/ppermute | solution.py:24
  84.2 3.3 %collective-permute-start.11 = (bf16[80,6]{0,1:T(8,128)(2,1)S(1)}, bf16[80,6]{0,1:T(8,128)(2,1)S(1)}, u32[]{:S(2)}, u32[]{:S(2)}) collective-permute-start(bf16[80,6]{0,1:T(8,128)(2,1)S(1)} %bitcast.155), channel_id=1, source_target_pairs={{0,1},{1,2},{2,3},{4,5},{5,6},{6,7},{8,9},{9,10},{10,11},{12,13},{... | collective-permute-start | bytes 2888 | tf_op jit(solution)/shard_map/ppermute | solution.py:25
  87.9 1.9 %collective-permute-start.10 = (bf16[80,6]{0,1:T(8,128)(2,1)S(1)}, bf16[80,6]{0,1:T(8,128)(2,1)S(1)}, u32[]{:S(2)}, u32[]{:S(2)}) collective-permute-start(bf16[80,6]{0,1:T(8,128)(2,1)S(1)} %bitcast.157), channel_id=1, source_target_pairs={{1,0},{2,1},{3,2},{5,4},{6,5},{7,6},{9,8},{10,9},{11,10},{13,12},{... | collective-permute-start | bytes 2888 | tf_op jit(solution)/shard_map/ppermute | solution.py:26
  89.9 1.1 fusion.131
  91.2 1.0 copy.136
  92.2 0.6 collective-permute-done.10
  93.3 0.9 convert_element_type.89
  94.2 0.8 convert_element_type.88
  95.1 1.3 %fusion.147 = (bf16[2304,80]{0,1:T(8,128)(2,1)S(1)}, f32[2304,80]{0,1:T(8,128)S(1)}) fusion(f32[80,80]{1,0:T(8,128)S(1)} %copy-done, f32[80,2304]{1,0:T(8,128)S(1)} %fusion.148, f32[80,2304]{1,0:T(8,128)S(1)} %get-tuple-element.50, f32[80,1920]{1,0:T(8,128)S(1)} %copy-done.10, f32[80,384]{1,0:T(8,128)S(1)} %convert_element_type.89, ...), kind=kOutput, calls=%fused_computation.223 | convolution fusion | flops 180080640 | bytes 7052800 | tf_op jit(solution)/shard_map/dot_general | solution.py:73
  96.5 1.2 %fusion.9 = f32[80,256]{1,0:T(8,128)S(1)} fusion(f32[80,256]{1,0:T(8,128)S(1)} %fusion.101, f32[2304,80]{0,1:T(8,128)S(1)} %get-tuple-element.52, pred[256,2304]{1,0:T(32,128)(4,1)S(1)} %copy-done.5), kind=kOutput, calls=%fused_computation.24 | convolution fusion | flops 566272000 | bytes 1490944 | tf_op jit(solution)/shard_map/dot_general | solution.py:149
  97.7 0.8 broadcast_select_fusion
  98.5 4.7 %all-to-all-start.2 = ((f32[80,4,256]{2,0,1:T(8,128)}), f32[80,4,256]{2,0,1:T(8,128)S(1)}, u32[]{:S(2)}, u32[]{:S(2)}) async-start(f32[80,4,256]{2,0,1:T(8,128)} %broadcast_select_fusion), calls=%async_computation.2 | async-start | bytes 655360 | tf_op jit(solution)/shard_map/all_to_all | solution.py:163
  103.2 0.8 copy.148
  103.9 8.7 %all-to-all-done.2 = f32[80,4,256]{2,0,1:T(8,128)S(1)} async-done(((f32[80,4,256]{2,0,1:T(8,128)}), f32[80,4,256]{2,0,1:T(8,128)S(1)}, u32[]{:S(2)}, u32[]{:S(2)}) %all-to-all-start.2) | async-done | bytes 327712 | tf_op jit(solution)/shard_map/all_to_all | solution.py:163
  112.9 6.3 %scatter_custom_fusion = f32[80,2048]{0,1:T(8,128)S(1)} fusion(s32[1024]{0:T(1024)S(1)} %bitcast.147, f32[1024,80]{1,0:T(8,128)S(1)} %copy.109, f32[]{:T(128)} %constant.109.clone.1), kind=kCustom, calls=%fused_computation.92 | custom fusion | flops 81920 | bytes 655364 | tf_op jit(solution)/shard_map/scatter-add | solution.py:164
  119.2 0.3 copy.110
  119.5 0.7 copy-done.3
  120.4 0.8 copy.137
  (132 shorter events, 6.6 us)
Async XLA Ops:
  0.6 33.1 %copy-start = (f32[80,80]{1,0:T(8,128)S(1)}, f32[80,80]{1,0:T(8,128)}, u32[]{:S(2)}) copy-start(f32[80,80]{1,0:T(8,128)} %param.16) | copy-start | bytes 76804
  0.6 10.2 %copy-start.15 = (bf16[80,6,384]{2,0,1:T(8,128)(2,1)S(1)}, bf16[80,6,384]{2,0,1:T(8,128)(2,1)}, u32[]{:S(2)}) copy-start(bf16[80,6,384]{2,0,1:T(8,128)(2,1)} %param.11) | copy-start | bytes 1105924
  0.7 10.3 %copy-start.14 = (bf16[80,8,256]{2,1,0:T(8,128)(2,1)S(1)}, bf16[80,8,256]{2,1,0:T(8,128)(2,1)}, u32[]{:S(2)}) copy-start(bf16[80,8,256]{2,1,0:T(8,128)(2,1)} %param.10) | copy-start | bytes 983044
  3.5 14.6 %copy-start.20 = (s32[1,1,256,1]{2,3,1,0:T(1,128)S(1)}, s32[1,1,256,1]{2,3,1,0:T(1,128)}, u32[]{:S(2)}) copy-start(s32[1,1,256,1]{2,3,1,0:T(1,128)} %param.17) | copy-start | bytes 3076
  3.5 14.6 %copy-start.21 = (s32[1,1,256]{2,1,0:T(1,128)S(1)}, s32[1,1,256]{2,1,0:T(1,128)}, u32[]{:S(2)}) copy-start(s32[1,1,256]{2,1,0:T(1,128)} %param.18) | copy-start | bytes 3076
  3.5 28.7 %collective-permute-start = (bf16[80,640]{1,0:T(8,128)(2,1)}, bf16[80,640]{1,0:T(8,128)(2,1)}, u32[]{:S(2)}, u32[]{:S(2)}) collective-permute-start(bf16[80,640]{1,0:T(8,128)(2,1)} %pad_maximum_fusion), channel_id=1, source_target_pairs={{4,0},{8,4},{12,8},{5,1},{9,5},{13,9},{6,2},{10,6},{14,10},{7,3},{... | collective-permute-start | bytes 307208 | tf_op jit(solution)/shard_map/ppermute | solution.py:24
  5.6 27.4 %collective-permute-start.1 = (bf16[80,640]{1,0:T(8,128)(2,1)}, bf16[80,640]{1,0:T(8,128)(2,1)}, u32[]{:S(2)}, u32[]{:S(2)}) collective-permute-start(bf16[80,640]{1,0:T(8,128)(2,1)} %pad_maximum_fusion.1), channel_id=1, source_target_pairs={{0,4},{4,8},{8,12},{1,5},{5,9},{9,13},{2,6},{6,10},{10,14},{3,7},{... | collective-permute-start | bytes 307208 | tf_op jit(solution)/shard_map/ppermute | solution.py:23
  11.4 18.1 %collective-permute-start.3 = (bf16[80,14]{0,1:T(8,128)(2,1)S(1)}, bf16[80,14]{0,1:T(8,128)(2,1)S(1)}, u32[]{:S(2)}, u32[]{:S(2)}) collective-permute-start(bf16[80,14]{0,1:T(8,128)(2,1)S(1)} %pad_maximum_fusion.3), channel_id=1, source_target_pairs={{0,1},{1,2},{2,3},{4,5},{5,6},{6,7},{8,9},{9,10},{10,11},{12,13},{... | collective-permute-start | bytes 6728 | tf_op jit(solution)/shard_map/ppermute | solution.py:25
  16.1 13.4 %collective-permute-start.2 = (bf16[80,14]{0,1:T(8,128)(2,1)S(1)}, bf16[80,14]{0,1:T(8,128)(2,1)S(1)}, u32[]{:S(2)}, u32[]{:S(2)}) collective-permute-start(bf16[80,14]{0,1:T(8,128)(2,1)S(1)} %pad_maximum_fusion.2), channel_id=1, source_target_pairs={{1,0},{2,1},{3,2},{5,4},{6,5},{7,6},{9,8},{10,9},{11,10},{13,12},{... | collective-permute-start | bytes 6728 | tf_op jit(solution)/shard_map/ppermute | solution.py:26
  18.7 13.4 %all-to-all-start = ((s32[4,256,1]{1,2,0:T(1,128)}), s32[4,256,1]{1,2,0:T(1,128)S(1)}, u32[]{:S(2)}, u32[]{:S(2)}) async-start(s32[4,256,1]{1,2,0:T(1,128)} %compare_select_fusion.1), calls=%async_computation | async-start | bytes 8192 | tf_op jit(solution)/shard_map/all_to_all | solution.py:120
  25.0 1.4 %copy-start.1 = (s32[24]{0:T(128)S(1)}, s32[24]{0:T(128)}, u32[]{:S(2)}) copy-start(s32[24]{0:T(128)} %param.19) | copy-start | bytes 292
  30.9 2.8 %copy-start.22 = (f32[80]{0:T(128)S(1)}, f32[80]{0:T(128)}, u32[]{:S(2)}) copy-start(f32[80]{0:T(128)} %param.12) | copy-start | bytes 964
  36.6 3.2 %copy-start.2 = (f32[80,2048]{1,0:T(8,128)}, f32[80,2048]{1,0:T(8,128)S(1)}, u32[]{:S(2)}) copy-start(f32[80,2048]{1,0:T(8,128)S(1)} %convolution_bitcast_fusion.2) | copy-start | bytes 1966084
  40.7 14.1 %all-to-all-start.1 = ((f32[80,4,256]{2,0,1:T(8,128)}), f32[80,4,256]{2,0,1:T(8,128)S(1)}, u32[]{:S(2)}, u32[]{:S(2)}) async-start(f32[80,4,256]{2,0,1:T(8,128)} %broadcast_select_fusion.1), calls=%async_computation.1 | async-start | bytes 655360 | tf_op jit(solution)/shard_map/all_to_all | solution.py:121
  46.8 8.0 %copy-start.4 = (pred[256,2304]{1,0:T(32,128)(4,1)S(1)}, pred[256,2304]{1,0:T(32,128)(4,1)}, u32[]{:S(2)}) copy-start(pred[256,2304]{1,0:T(32,128)(4,1)} %fusion.6) | copy-start | bytes 1769476
  49.3 6.4 %copy-start.6 = (f32[80,2303]{1,0:T(8,128)S(1)}, f32[80,2303]{1,0:T(8,128)}, u32[]{:S(2)}) copy-start(f32[80,2303]{1,0:T(8,128)} %get-tuple-element.21) | copy-start | bytes 2210884
  49.3 6.4 %copy-start.18 = (f32[80]{0:T(128)S(1)}, f32[80]{0:T(128)}, u32[]{:S(2)}) copy-start(f32[80]{0:T(128)} %param.14) | copy-start | bytes 964
  49.3 6.4 %copy-start.19 = (f32[80]{0:T(128)S(1)}, f32[80]{0:T(128)}, u32[]{:S(2)}) copy-start(f32[80]{0:T(128)} %param.13) | copy-start | bytes 964
  54.8 0.9 copy-start.16
  54.8 1.0 copy-start.17
  59.7 13.8 %collective-permute-start.5 = (bf16[80,384]{1,0:T(8,128)(2,1)S(1)}, bf16[80,384]{1,0:T(8,128)(2,1)S(1)}, u32[]{:S(2)}, u32[]{:S(2)}) collective-permute-start(bf16[80,384]{1,0:T(8,128)(2,1)S(1)} %bitcast.142), channel_id=1, source_target_pairs={{0,4},{4,8},{8,12},{1,5},{5,9},{9,13},{2,6},{6,10},{10,14},{3,7},{... | collective-permute-start | bytes 184328 | tf_op jit(solution)/shard_map/ppermute | solution.py:23
  61.1 12.5 %collective-permute-start.4 = (bf16[80,384]{1,0:T(8,128)(2,1)S(1)}, bf16[80,384]{1,0:T(8,128)(2,1)S(1)}, u32[]{:S(2)}, u32[]{:S(2)}) collective-permute-start(bf16[80,384]{1,0:T(8,128)(2,1)S(1)} %bitcast.144), channel_id=1, source_target_pairs={{4,0},{8,4},{12,8},{5,1},{9,5},{13,9},{6,2},{10,6},{14,10},{7,3},{... | collective-permute-start | bytes 184328 | tf_op jit(solution)/shard_map/ppermute | solution.py:24
  62.5 8.7 %collective-permute-start.7 = (bf16[80,6]{0,1:T(8,128)(2,1)S(1)}, bf16[80,6]{0,1:T(8,128)(2,1)S(1)}, u32[]{:S(2)}, u32[]{:S(2)}) collective-permute-start(bf16[80,6]{0,1:T(8,128)(2,1)S(1)} %bitcast.154), channel_id=1, source_target_pairs={{0,1},{1,2},{2,3},{4,5},{5,6},{6,7},{8,9},{9,10},{10,11},{12,13},{... | collective-permute-start | bytes 2888 | tf_op jit(solution)/shard_map/ppermute | solution.py:25
  68.2 4.9 %collective-permute-start.6 = (bf16[80,6]{0,1:T(8,128)(2,1)S(1)}, bf16[80,6]{0,1:T(8,128)(2,1)S(1)}, u32[]{:S(2)}, u32[]{:S(2)}) collective-permute-start(bf16[80,6]{0,1:T(8,128)(2,1)S(1)} %bitcast.156), channel_id=1, source_target_pairs={{1,0},{2,1},{3,2},{5,4},{6,5},{7,6},{9,8},{10,9},{11,10},{13,12},{... | collective-permute-start | bytes 2888 | tf_op jit(solution)/shard_map/ppermute | solution.py:26
  73.2 1.1 copy-start.13
  73.4 1.2 copy-start.7
  73.4 1.4 %copy-start.9 = (f32[10,8,6,384]{3,1,2,0:T(8,128)S(1)}, f32[10,8,6,384]{3,1,2,0:T(8,128)}, u32[]{:S(2)}) copy-start(f32[10,8,6,384]{3,1,2,0:T(8,128)} %copy.134) | copy-start | bytes 2211844
  73.4 1.6 %copy-start.12 = (f32[80,1920]{1,0:T(8,128)S(1)}, f32[80,1920]{1,0:T(8,128)}, u32[]{:S(2)}) copy-start(f32[80,1920]{1,0:T(8,128)} %get-tuple-element.19) | copy-start | bytes 1843204
  77.0 16.3 %collective-permute-start.9 = (bf16[80,384]{1,0:T(8,128)(2,1)S(1)}, bf16[80,384]{1,0:T(8,128)(2,1)}, u32[]{:S(2)}, u32[]{:S(2)}) collective-permute-start(bf16[80,384]{1,0:T(8,128)(2,1)S(1)} %bitcast.143), channel_id=1, source_target_pairs={{0,4},{4,8},{8,12},{1,5},{5,9},{9,13},{2,6},{6,10},{10,14},{3,7},{... | collective-permute-start | bytes 184328 | tf_op jit(solution)/shard_map/ppermute | solution.py:23
  82.5 11.7 %collective-permute-start.8 = (bf16[80,384]{1,0:T(8,128)(2,1)}, bf16[80,384]{1,0:T(8,128)(2,1)}, u32[]{:S(2)}, u32[]{:S(2)}) collective-permute-start(bf16[80,384]{1,0:T(8,128)(2,1)} %bitcast.105), channel_id=1, source_target_pairs={{4,0},{8,4},{12,8},{5,1},{9,5},{13,9},{6,2},{10,6},{14,10},{7,3},{... | collective-permute-start | bytes 184328 | tf_op jit(solution)/shard_map/ppermute | solution.py:24
  84.2 6.8 %collective-permute-start.11 = (bf16[80,6]{0,1:T(8,128)(2,1)S(1)}, bf16[80,6]{0,1:T(8,128)(2,1)S(1)}, u32[]{:S(2)}, u32[]{:S(2)}) collective-permute-start(bf16[80,6]{0,1:T(8,128)(2,1)S(1)} %bitcast.155), channel_id=1, source_target_pairs={{0,1},{1,2},{2,3},{4,5},{5,6},{6,7},{8,9},{9,10},{10,11},{12,13},{... | collective-permute-start | bytes 2888 | tf_op jit(solution)/shard_map/ppermute | solution.py:25
  87.9 4.9 %collective-permute-start.10 = (bf16[80,6]{0,1:T(8,128)(2,1)S(1)}, bf16[80,6]{0,1:T(8,128)(2,1)S(1)}, u32[]{:S(2)}, u32[]{:S(2)}) collective-permute-start(bf16[80,6]{0,1:T(8,128)(2,1)S(1)} %bitcast.157), channel_id=1, source_target_pairs={{1,0},{2,1},{3,2},{5,4},{6,5},{7,6},{9,8},{10,9},{11,10},{13,12},{... | collective-permute-start | bytes 2888 | tf_op jit(solution)/shard_map/ppermute | solution.py:26
  93.1 2.0 %copy-start.8 = (f32[10,8,6,384]{3,1,2,0:T(8,128)S(1)}, f32[10,8,6,384]{3,1,2,0:T(8,128)}, u32[]{:S(2)}) copy-start(f32[10,8,6,384]{3,1,2,0:T(8,128)} %copy.136) | copy-start | bytes 2211844
  93.1 2.0 %copy-start.10 = (f32[80,1920]{1,0:T(8,128)S(1)}, f32[80,1920]{1,0:T(8,128)}, u32[]{:S(2)}) copy-start(f32[80,1920]{1,0:T(8,128)} %get-tuple-element.15) | copy-start | bytes 1843204
  93.1 2.0 %copy-start.11 = (f32[80,1920]{1,0:T(8,128)S(1)}, f32[80,1920]{1,0:T(8,128)}, u32[]{:S(2)}) copy-start(f32[80,1920]{1,0:T(8,128)} %get-tuple-element.16) | copy-start | bytes 1843204
  95.1 1.4 %copy-start.5 = (pred[256,2304]{1,0:T(32,128)(4,1)S(1)}, pred[256,2304]{1,0:T(32,128)(4,1)}, u32[]{:S(2)}) copy-start(pred[256,2304]{1,0:T(32,128)(4,1)} %fusion.6) | copy-start | bytes 1769476
  98.5 14.2 %all-to-all-start.2 = ((f32[80,4,256]{2,0,1:T(8,128)}), f32[80,4,256]{2,0,1:T(8,128)S(1)}, u32[]{:S(2)}, u32[]{:S(2)}) async-start(f32[80,4,256]{2,0,1:T(8,128)} %broadcast_select_fusion), calls=%async_computation.2 | async-start | bytes 655360 | tf_op jit(solution)/shard_map/all_to_all | solution.py:163
  119.2 1.1 copy-start.3
  119.2 1.1 copy-start.23
where the time goes:
time: 122 us; the launch traced here: 121 us
  starting transfers between devices  46.3 us (38%)
  local copies, waits for them, and re-layouts  30.1 us (25%)
  other arithmetic  18.7 us (15%)
  waiting for transfers between devices  13.9 us (11%)
  matrix products  10.8 us (9%)
  between operations  1.45 us (1%)
    ppermute x3, starting transfers between devices, exchange(): left = lax.ppermute(last_cols, Y_AXES, fwd_y)  12.1 us
    ppermute x3, starting transfers between devices, exchange(): above = lax.ppermute(last_rows, 'gx', fwd_x)  11.5 us
    unnamed x68, local copies, waits for them, and re-layouts  10.8 us
    all_to_all x1, waiting for transfers between devices, body(): lax.all_to_all(outgoing, 'gx', split_axis=1, concat_axis=1, tiled=True)  8.71 us
    dot_general x4, matrix products, mix_levels(): jnp.dot(matrix, flat, precision=HI, preferred_element_type=jnp.float32)  8.71 us
    convert_element_type x12, other arithmetic, flat_stencil(): above, below, left, right = (h.astype(flat.dtype) for h in halo)  6.43 us
    scatter-add x1, other arithmetic, body(): summed = jnp.zeros_like(flat_parent).at[:, served_ids].add(incoming)  6.28 us
    ppermute x3, starting transfers between devices, exchange(): right = lax.ppermute(first_cols, Y_AXES, bwd_y)  5.74 us
  transfers between devices with their start and end apart: 15, of which 4 were waited for; matrix products, arithmetic and copies ran while one was open for 23% of the time, Pallas kernels for 0%

commit v1 on v0

--- a/solution.py
+++ b/solution.py
@@ -5,6 +5,18 @@
 
 Y_AXES = ("gy", "gz")
 HI = lax.Precision.HIGHEST
+
+
+def split_up(x, dim, size):
+    dims = x.shape
+    blocks = x.reshape(*dims[:dim], size, dims[dim] // size, *dims[dim + 1 :])
+    return jnp.moveaxis(blocks, dim, 0)
+
+
+def in_order(parts, dim):
+    parts = jnp.moveaxis(parts, 0, dim)
+    lengths = parts.shape
+    return parts.reshape(*lengths[:dim], lengths[dim] * lengths[dim + 1], *lengths[dim + 2 :])
 
 
 def shift_pairs(count):
@@ -118,9 +130,17 @@
         places = owners * slots + order_in
         wanted = jnp.zeros((tiles_x * slots,), jnp.int32).at[places].set(cells)
     served_ids = lax.all_to_all(wanted, "gx", split_axis=0, concat_axis=0, tiled=True)
-    answers = lax.all_to_all(
-        jnp.take(flat_parent, served_ids, axis=1), "gx", split_axis=1, concat_axis=1, tiled=True
-    )
+    shard = jnp.take(flat_parent, served_ids, axis=1)
+    count_2, here = (lax.axis_size("gx"), lax.axis_index("gx"))
+    pieces = split_up(shard, 1, count_2)
+    outs = [pieces[here]]
+    for step in range(1, count_2):
+        sent = pieces[(here + step) % count_2]
+        outs.append(
+            lax.ppermute(sent, "gx", [(i_2, (i_2 + step) % count_2) for i_2 in range(count_2)])
+        )
+    pieces = jnp.stack(outs)[(here - jnp.arange(count_2)) % count_2]
+    answers = in_order(pieces, 1)
     if slots >= requests:
         answers = answers.reshape(levels, tiles_x, slots)[:, :, :requests]
         forcing_flat = answers[:, 0, :]

time: 122 us -> 118 us (0.967)
  other arithmetic: 18.7 us -> 11.9 us
  local copies, waits for them, and re-layouts: 30.1 us -> 32.6 us
    convert_element_type x12, other arithmetic: 6.43 us -> 1.39 us  [flat_stencil(): above, below, left, right = (h.astype(flat.dtype) for h in halo)]
    ppermute x0 -> x3, starting transfers between devices: none -> 4.9 us  [body(): lax.ppermute(sent, 'gx', [(i_2, (i_2 + step) % count_2) for i_2 in range(...]
    all_to_all x1 -> x0, starting transfers between devices: 4.54 us -> none  [body(): lax.all_to_all(jnp.take(flat_parent, served_ids, axis=1), 'gx', split_axi...]
    all_to_all x1 -> x0, waiting for transfers between devices: 3.94 us -> none  [body(): lax.all_to_all(jnp.take(flat_parent, served_ids, axis=1), 'gx', split_axi...]
    ppermute x0 -> x3, waiting for transfers between devices: none -> 3.24 us  [body(): lax.ppermute(sent, 'gx', [(i_2, (i_2 + step) % count_2) for i_2 in range(...]
    slice x6, local copies, waits for them, and re-layouts: 0.79 us -> 2.83 us  [exchange(): first_cols = jnp.concatenate([b[:, :, 0] for b in blocks], axis=1)]
    all_to_all x1, starting transfers between devices: 3.58 us -> 5.38 us  [body(): lax.all_to_all(wanted, 'gx', split_axis=0, concat_axis=0, tiled=True)]
    unnamed x68 -> x80, local copies, waits for them, and re-layouts: 10.8 us -> 12.5 us
  transfers between devices with their start and end apart: 15 -> 17, of which waited for: 4 -> 2; matrix products, arithmetic and copies ran while one was open for 23% -> 20% of each run, Pallas kernels for 0% -> 0%
where the time goes in v1:
time: 118 us; the launch traced here: 116 us
  starting transfers between devices  47.1 us (40%)
  local copies, waits for them, and re-layouts  32.6 us (28%)
  waiting for transfers between devices  12.9 us (11%)
  other arithmetic  11.9 us (10%)
  matrix products  10.3 us (9%)
  between operations  1.65 us (1%)
    unnamed x80, local copies, waits for them, and re-layouts  12.5 us
    ppermute x3, starting transfers between devices, exchange(): above = lax.ppermute(last_rows, 'gx', fwd_x)  11.9 us
    ppermute x3, starting transfers between devices, exchange(): left = lax.ppermute(last_cols, Y_AXES, fwd_y)  10.9 us
    all_to_all x1, waiting for transfers between devices, body(): lax.all_to_all(outgoing, 'gx', split_axis=1, concat_axis=1, tiled=True)  9.61 us
    dot_general x4, matrix products, mix_levels(): jnp.dot(matrix, flat, precision=HI, preferred_element_type=jnp.float32)  8.25 us
    ppermute x3, starting transfers between devices, exchange(): right = lax.ppermute(first_cols, Y_AXES, bwd_y)  6.58 us
    scatter-add x1, other arithmetic, body(): summed = jnp.zeros_like(flat_parent).at[:, served_ids].add(incoming)  6.28 us
    all_to_all x1, starting transfers between devices, body(): lax.all_to_all(wanted, 'gx', split_axis=0, concat_axis=0, tiled=True)  5.38 us
  transfers between devices with their start and end apart: 17, of which 2 were waited for; matrix products, arithmetic and copies ran while one was open for 20% of the time, Pallas kernels for 0%

profile of v1, /device:TPU:1, one launch (start us, length us, event | category | flops | bytes accessed | tf_op | source)
XLA Modules:
  0.0 116.4 jit_solution(6867547979093723645)
XLA Ops:
  0.7 1.2 %fusion.145 = (bf16[80,8,1]{2,1,0:T(8,128)(2,1)S(1)}, bf16[80,8,1]{2,1,0:T(8,128)(2,1)S(1)}) fusion(bf16[80,8,256]{2,1,0:T(8,128)(2,1)} %param.10), kind=kLoop, calls=%fused_computation.232 | loop fusion | bytes 5120 | tf_op jit(solution)/shard_map/slice | solution.py:34
  2.0 1.1 fusion.144
  3.3 1.9 %collective-permute-start.2 = (bf16[80,14]{0,1:T(8,128)(2,1)S(1)}, bf16[80,14]{0,1:T(8,128)(2,1)S(1)}, u32[]{:S(2)}, u32[]{:S(2)}) collective-permute-start(bf16[80,14]{0,1:T(8,128)(2,1)S(1)} %pad_maximum_fusion.3), channel_id=1, source_target_pairs={{1,0},{2,1},{3,2},{5,4},{6,5},{7,6},{9,8},{10,9},{11,10},{13,12},{... | collective-permute-start | bytes 6728 | tf_op jit(solution)/shard_map/ppermute | solution.py:38
  5.5 4.5 %collective-permute-start.3 = (bf16[80,14]{0,1:T(8,128)(2,1)S(1)}, bf16[80,14]{0,1:T(8,128)(2,1)S(1)}, u32[]{:S(2)}, u32[]{:S(2)}) collective-permute-start(bf16[80,14]{0,1:T(8,128)(2,1)S(1)} %pad_maximum_fusion.4), channel_id=1, source_target_pairs={{0,1},{1,2},{2,3},{4,5},{5,6},{6,7},{8,9},{9,10},{10,11},{12,13},{... | collective-permute-start | bytes 6728 | tf_op jit(solution)/shard_map/ppermute | solution.py:37
  10.2 3.2 %collective-permute-start.1 = (bf16[80,640]{1,0:T(8,128)(2,1)S(1)}, bf16[80,640]{1,0:T(8,128)(2,1)S(1)}, u32[]{:S(2)}, u32[]{:S(2)}) collective-permute-start(bf16[80,640]{1,0:T(8,128)(2,1)S(1)} %pad_maximum_fusion.2), channel_id=1, source_target_pairs={{0,4},{4,8},{8,12},{1,5},{5,9},{9,13},{2,6},{6,10},{10,14},{3,7},{... | collective-permute-start | bytes 307208 | tf_op jit(solution)/shard_map/ppermute | solution.py:35
  13.5 1.3 %collective-permute-start = (bf16[80,640]{1,0:T(8,128)(2,1)S(1)}, bf16[80,640]{1,0:T(8,128)(2,1)S(1)}, u32[]{:S(2)}, u32[]{:S(2)}) collective-permute-start(bf16[80,640]{1,0:T(8,128)(2,1)S(1)} %pad_maximum_fusion.1), channel_id=1, source_target_pairs={{4,0},{8,4},{12,8},{5,1},{9,5},{13,9},{6,2},{10,6},{14,10},{7,3},{... | collective-permute-start | bytes 307208 | tf_op jit(solution)/shard_map/ppermute | solution.py:36
  14.8 0.6 compare_select_fusion.1
  15.4 5.4 %all-to-all-start = ((s32[4,256,1]{1,2,0:T(1,128)}), s32[4,256,1]{1,2,0:T(1,128)S(1)}, u32[]{:S(2)}, u32[]{:S(2)}) async-start(s32[4,256,1]{1,2,0:T(1,128)} %compare_select_fusion.1), calls=%async_computation | async-start | bytes 8192 | tf_op jit(solution)/shard_map/all_to_all | solution.py:132
  20.8 0.2 fusion.138
  21.1 1.1 fusion.139
  22.4 1.4 %fusion.136 = (f32[80,2303]{1,0:T(8,128)}, f32[80,2303]{1,0:T(8,128)}) fusion(f32[80,2304]{1,0:T(8,128)S(1)} %bitcast.120), kind=kLoop, calls=%fused_computation.223 | loop fusion | bytes 2947840 | tf_op jit(solution)/shard_map/slice | solution.py:76
  23.8 1.2 fusion.137
  25.0 0.6 gather_fusion
  25.8 2.2 %fusion.6 = pred[256,2304]{1,0:T(32,128)(4,1)} fusion(s32[256]{0:T(256)S(1)} %get-tuple-element.62, s32[256]{0:T(256)S(1)} %get-tuple-element.63, s32[2304]{0:T(1024)S(1)} %get-tuple-element.66, s32[2304]{0:T(1024)S(1)} %get-tuple-element.67, s32[256]{0:T(256)S(1)} %get-tuple-element.61, s32[256]{0:T(256)S(1)} %get-tuple-element.64, ...), kind=kLoop, calls=%fused_computation.21 | loop fusion | flops 13565952 | bytes 635904 | tf_op jit(solution)/shard_map/and | solution.py:103
  28.4 1.0 copy.133
  29.6 1.0 copy.134
  30.9 1.0 copy.135
  32.2 1.0 copy.136
  33.3 0.6 copy-done.20
  34.0 2.8 %convolution_bitcast_fusion.2 = f32[80,2048]{1,0:T(8,128)S(1)} fusion(f32[80,80]{1,0:T(8,128)S(1)} %copy-done, f32[80,2048]{1,0:T(8,128)S(1)} %bitcast.125, f32[80,256]{1,0:T(8,128)S(1)} %slice_convert_fusion.3, f32[80,1792]{1,0:T(8,128)} %get-tuple-element.28, f32[80,1792]{1,0:T(8,128)} %get-tuple-element.27, f32[80,256]{1,0:T(8,128)S(1)} %slice_convert_fusion.2, ...), kind=kOutput, calls=%fused_computation.14 | convolution fusion | flops 159088640 | bytes 5272256 | tf_op jit(solution)/shard_map/dot_general | solution.py:85
  36.7 0.3 copy.97
  37.1 2.8 %gather_fusion.1 = f32[1024,80]{1,0:T(8,128)S(1)} fusion(f32[80,2048]{0,1:T(8,128)S(1)} %copy.97, s32[1024]{0:T(1024)S(1)} %broadcast_clamp_fusion), kind=kCustom, calls=%fused_computation.1 | custom fusion | bytes 659456 | tf_op jit(solution)/shard_map/jit(_take)/gather | solution.py:133
  40.3 1.5 %collective-permute-start.4 = (f32[80,256]{1,0:T(8,128)S(1)}, f32[80,256]{1,0:T(8,128)S(1)}, u32[]{:S(2)}, u32[]{:S(2)}) collective-permute-start(f32[80,256]{1,0:T(8,128)S(1)} %bitcast.157), channel_id=1, source_target_pairs={{0,4},{4,8},{8,12},{12,0},{1,5},{5,9},{9,13},{13,1},{2,6},{6,10},{... | collective-permute-start | bytes 245768 | tf_op jit(solution)/shard_map/ppermute | solution.py:140
  41.9 2.1 %collective-permute-start.5 = (f32[80,256]{1,0:T(8,128)S(1)}, f32[80,256]{1,0:T(8,128)S(1)}, u32[]{:S(2)}, u32[]{:S(2)}) collective-permute-start(f32[80,256]{1,0:T(8,128)S(1)} %bitcast.158), channel_id=1, source_target_pairs={{0,8},{4,12},{8,0},{12,4},{1,9},{5,13},{9,1},{13,5},{2,10},{6,14},... | collective-permute-start | bytes 245768 | tf_op jit(solution)/shard_map/ppermute | solution.py:140
  44.1 1.2 %collective-permute-start.6 = (f32[80,256]{1,0:T(8,128)S(1)}, f32[80,256]{1,0:T(8,128)S(1)}, u32[]{:S(2)}, u32[]{:S(2)}) collective-permute-start(f32[80,256]{1,0:T(8,128)S(1)} %bitcast.159), channel_id=1, source_target_pairs={{0,12},{4,0},{8,4},{12,8},{1,13},{5,1},{9,5},{13,9},{2,14},{6,2},{... | collective-permute-start | bytes 245768 | tf_op jit(solution)/shard_map/ppermute | solution.py:140
  45.4 0.7 slice_convert_fusion
  46.0 0.7 slice_convert_fusion.1
  46.8 3.2 %collective-permute-done.5 = f32[80,256]{1,0:T(8,128)S(1)} collective-permute-done((f32[80,256]{1,0:T(8,128)S(1)}, f32[80,256]{1,0:T(8,128)S(1)}, u32[]{:S(2)}, u32[]{:S(2)}) %collective-permute-start.5) | collective-permute-done | bytes 81952 | tf_op jit(solution)/shard_map/ppermute | solution.py:140
  50.1 0.6 gather_fusion.2
  50.8 0.8 fusion.150
  51.6 0.2 copy-done.6
  51.8 0.2 copy-done.7
  52.1 2.8 %fusion.147 = (bf16[80,2304]{1,0:T(8,128)(2,1)S(1)}, f32[80,2304]{1,0:T(8,128)S(1)}) fusion(f32[80,80]{1,0:T(8,128)S(1)} %copy-done, f32[80,2304]{1,0:T(8,128)S(1)} %fusion.150, f32[80,2304]{1,0:T(8,128)S(1)} %bitcast.122, f32[80,1920]{1,0:T(8,128)} %get-tuple-element.23, f32[80,384]{1,0:T(8,128)S(1)} %copy-done.18, f32[80,384]{1,0:T(8,128)S(1)} %copy-done.19, ...), kind=kOutput, calls=%fused_computation.234 | convolution fusion | flops 180080640 | bytes 7052800 | tf_op jit(solution)/shard_map/dot_general | solution.py:85
  54.9 0.4 reshape.342
  55.8 2.7 %collective-permute-start.9 = (bf16[80,6]{0,1:T(8,128)(2,1)S(1)}, bf16[80,6]{0,1:T(8,128)(2,1)S(1)}, u32[]{:S(2)}, u32[]{:S(2)}) collective-permute-start(bf16[80,6]{0,1:T(8,128)(2,1)S(1)} %bitcast.175), channel_id=1, source_target_pairs={{1,0},{2,1},{3,2},{5,4},{6,5},{7,6},{9,8},{10,9},{11,10},{13,12},{... | collective-permute-start | bytes 2888 | tf_op jit(solution)/shard_map/ppermute | solution.py:38
  58.7 2.8 %collective-permute-start.10 = (bf16[80,6]{0,1:T(8,128)(2,1)S(1)}, bf16[80,6]{0,1:T(8,128)(2,1)S(1)}, u32[]{:S(2)}, u32[]{:S(2)}) collective-permute-start(bf16[80,6]{0,1:T(8,128)(2,1)S(1)} %bitcast.173), channel_id=1, source_target_pairs={{0,1},{1,2},{2,3},{4,5},{5,6},{6,7},{8,9},{9,10},{10,11},{12,13},{... | collective-permute-start | bytes 2888 | tf_op jit(solution)/shard_map/ppermute | solution.py:37
  61.5 1.1 fusion.134
  62.7 1.3 %collective-permute-start.7 = (bf16[80,384]{1,0:T(8,128)(2,1)S(1)}, bf16[80,384]{1,0:T(8,128)(2,1)S(1)}, u32[]{:S(2)}, u32[]{:S(2)}) collective-permute-start(bf16[80,384]{1,0:T(8,128)(2,1)S(1)} %bitcast.160), channel_id=1, source_target_pairs={{4,0},{8,4},{12,8},{5,1},{9,5},{13,9},{6,2},{10,6},{14,10},{7,3},{... | collective-permute-start | bytes 184328 | tf_op jit(solution)/shard_map/ppermute | solution.py:36
  64.0 4.8 %collective-permute-start.8 = (bf16[80,384]{1,0:T(8,128)(2,1)S(1)}, bf16[80,384]{1,0:T(8,128)(2,1)S(1)}, u32[]{:S(2)}, u32[]{:S(2)}) collective-permute-start(bf16[80,384]{1,0:T(8,128)(2,1)S(1)} %bitcast.162), channel_id=1, source_target_pairs={{0,4},{4,8},{8,12},{1,5},{5,9},{9,13},{2,6},{6,10},{10,14},{3,7},{... | collective-permute-start | bytes 184328 | tf_op jit(solution)/shard_map/ppermute | solution.py:35
  68.8 1.1 fusion.135
  70.1 1.0 copy.137
  71.6 0.7 copy-done.15
  72.3 0.3 copy-done.9
  72.6 0.2 copy-done.11
  73.0 1.3 %fusion.148 = (bf16[80,2304]{1,0:T(8,128)(2,1)S(1)}, f32[80,2304]{1,0:T(8,128)S(1)}) fusion(f32[80,80]{1,0:T(8,128)S(1)} %copy-done, f32[80,2304]{1,0:T(8,128)S(1)} %fusion.150, f32[80,2304]{1,0:T(8,128)S(1)} %get-tuple-element.52, f32[80,1920]{1,0:T(8,128)S(1)} %copy-done.14, f32[80,384]{1,0:T(8,128)S(1)} %convert_element_type.84, ...), kind=kOutput, calls=%fused_computation.235 | convolution fusion | flops 180080640 | bytes 7052800 | tf_op jit(solution)/shard_map/dot_general | solution.py:85
  74.3 0.4 reshape.345
  75.2 1.9 %collective-permute-start.13 = (bf16[80,6]{0,1:T(8,128)(2,1)S(1)}, bf16[80,6]{0,1:T(8,128)(2,1)S(1)}, u32[]{:S(2)}, u32[]{:S(2)}) collective-permute-start(bf16[80,6]{0,1:T(8,128)(2,1)S(1)} %bitcast.176), channel_id=1, source_target_pairs={{1,0},{2,1},{3,2},{5,4},{6,5},{7,6},{9,8},{10,9},{11,10},{13,12},{... | collective-permute-start | bytes 2888 | tf_op jit(solution)/shard_map/ppermute | solution.py:38
  77.3 3.6 %collective-permute-start.14 = (bf16[80,6]{0,1:T(8,128)(2,1)S(1)}, bf16[80,6]{0,1:T(8,128)(2,1)S(1)}, u32[]{:S(2)}, u32[]{:S(2)}) collective-permute-start(bf16[80,6]{0,1:T(8,128)(2,1)S(1)} %bitcast.174), channel_id=1, source_target_pairs={{0,1},{1,2},{2,3},{4,5},{5,6},{6,7},{8,9},{9,10},{10,11},{12,13},{... | collective-permute-start | bytes 2888 | tf_op jit(solution)/shard_map/ppermute | solution.py:37
  80.9 0.3 fusion.132
  81.2 1.3 %collective-permute-start.11 = (bf16[80,384]{1,0:T(8,128)(2,1)S(1)}, bf16[80,384]{1,0:T(8,128)(2,1)S(1)}, u32[]{:S(2)}, u32[]{:S(2)}) collective-permute-start(bf16[80,384]{1,0:T(8,128)(2,1)S(1)} %bitcast.161), channel_id=1, source_target_pairs={{4,0},{8,4},{12,8},{5,1},{9,5},{13,9},{6,2},{10,6},{14,10},{7,3},{... | collective-permute-start | bytes 184328 | tf_op jit(solution)/shard_map/ppermute | solution.py:36
  82.5 4.0 %collective-permute-start.12 = (bf16[80,384]{1,0:T(8,128)(2,1)S(1)}, bf16[80,384]{1,0:T(8,128)(2,1)S(1)}, u32[]{:S(2)}, u32[]{:S(2)}) collective-permute-start(bf16[80,384]{1,0:T(8,128)(2,1)S(1)} %bitcast.163), channel_id=1, source_target_pairs={{0,4},{4,8},{8,12},{1,5},{5,9},{9,13},{2,6},{6,10},{10,14},{3,7},{... | collective-permute-start | bytes 184328 | tf_op jit(solution)/shard_map/ppermute | solution.py:35
  86.5 1.1 fusion.133
  87.9 1.0 copy.139
  89.4 0.9 copy-done.10
  90.7 1.3 %fusion.149 = (bf16[2304,80]{0,1:T(8,128)(2,1)S(1)}, f32[2304,80]{0,1:T(8,128)S(1)}) fusion(f32[80,80]{1,0:T(8,128)S(1)} %copy-done, f32[80,2304]{1,0:T(8,128)S(1)} %fusion.150, f32[80,2304]{1,0:T(8,128)S(1)} %get-tuple-element.54, f32[80,1920]{1,0:T(8,128)S(1)} %copy-done.12, f32[80,384]{1,0:T(8,128)S(1)} %convert_element_type.89, ...), kind=kOutput, calls=%fused_computation.236 | convolution fusion | flops 180080640 | bytes 7052800 | tf_op jit(solution)/shard_map/dot_general | solution.py:85
  92.0 1.2 %fusion.9 = f32[80,256]{1,0:T(8,128)S(1)} fusion(f32[80,256]{1,0:T(8,128)S(1)} %fusion.101, f32[2304,80]{0,1:T(8,128)S(1)} %get-tuple-element.56, pred[256,2304]{1,0:T(32,128)(4,1)S(1)} %copy-done.5), kind=kOutput, calls=%fused_computation.25 | convolution fusion | flops 566272000 | bytes 1490944 | tf_op jit(solution)/shard_map/dot_general | solution.py:169
  93.3 0.8 broadcast_select_fusion.1
  94.0 3.5 %all-to-all-start.1 = ((f32[80,4,256]{2,0,1:T(8,128)}), f32[80,4,256]{2,0,1:T(8,128)S(1)}, u32[]{:S(2)}, u32[]{:S(2)}) async-start(f32[80,4,256]{2,0,1:T(8,128)} %broadcast_select_fusion.1), calls=%async_computation.1 | async-start | bytes 655360 | tf_op jit(solution)/shard_map/all_to_all | solution.py:183
  97.5 0.8 copy.152
  98.3 9.6 %all-to-all-done.1 = f32[80,4,256]{2,0,1:T(8,128)S(1)} async-done(((f32[80,4,256]{2,0,1:T(8,128)}), f32[80,4,256]{2,0,1:T(8,128)S(1)}, u32[]{:S(2)}, u32[]{:S(2)}) %all-to-all-start.1) | async-done | bytes 327712 | tf_op jit(solution)/shard_map/all_to_all | solution.py:183
  108.1 6.3 %scatter_custom_fusion = f32[80,2048]{0,1:T(8,128)S(1)} fusion(s32[1024]{0:T(1024)S(1)} %bitcast.166, f32[1024,80]{1,0:T(8,128)S(1)} %copy.115, f32[]{:T(128)} %constant.138.clone.1), kind=kCustom, calls=%fused_computation.93 | custom fusion | flops 81920 | bytes 655364 | tf_op jit(solution)/shard_map/scatter-add | solution.py:184
  114.4 0.3 copy.116
  114.7 0.7 copy-done.3
  115.6 0.8 copy.141
  (156 shorter events, 6.7 us)
Async XLA Ops:
  0.6 33.3 %copy-start = (f32[80,80]{1,0:T(8,128)S(1)}, f32[80,80]{1,0:T(8,128)}, u32[]{:S(2)}) copy-start(f32[80,80]{1,0:T(8,128)} %param.16) | copy-start | bytes 76804
  0.6 9.4 %copy-start.16 = (bf16[80,8,256]{2,1,0:T(8,128)(2,1)S(1)}, bf16[80,8,256]{2,1,0:T(8,128)(2,1)}, u32[]{:S(2)}) copy-start(bf16[80,8,256]{2,1,0:T(8,128)(2,1)} %param.10) | copy-start | bytes 983044
  0.7 9.5 %copy-start.17 = (bf16[80,6,384]{2,0,1:T(8,128)(2,1)S(1)}, bf16[80,6,384]{2,0,1:T(8,128)(2,1)}, u32[]{:S(2)}) copy-start(bf16[80,6,384]{2,0,1:T(8,128)(2,1)} %param.11) | copy-start | bytes 1105924
  2.0 12.7 %copy-start.26 = (s32[1,1,256,1]{2,3,1,0:T(1,128)S(1)}, s32[1,1,256,1]{2,3,1,0:T(1,128)}, u32[]{:S(2)}) copy-start(s32[1,1,256,1]{2,3,1,0:T(1,128)} %param.17) | copy-start | bytes 3076
  2.0 12.8 %copy-start.27 = (s32[1,1,256]{2,1,0:T(1,128)S(1)}, s32[1,1,256]{2,1,0:T(1,128)}, u32[]{:S(2)}) copy-start(s32[1,1,256]{2,1,0:T(1,128)} %param.18) | copy-start | bytes 3076
  3.3 24.8 %collective-permute-start.2 = (bf16[80,14]{0,1:T(8,128)(2,1)S(1)}, bf16[80,14]{0,1:T(8,128)(2,1)S(1)}, u32[]{:S(2)}, u32[]{:S(2)}) collective-permute-start(bf16[80,14]{0,1:T(8,128)(2,1)S(1)} %pad_maximum_fusion.3), channel_id=1, source_target_pairs={{1,0},{2,1},{3,2},{5,4},{6,5},{7,6},{9,8},{10,9},{11,10},{13,12},{... | collective-permute-start | bytes 6728 | tf_op jit(solution)/shard_map/ppermute | solution.py:38
  5.5 22.6 %collective-permute-start.3 = (bf16[80,14]{0,1:T(8,128)(2,1)S(1)}, bf16[80,14]{0,1:T(8,128)(2,1)S(1)}, u32[]{:S(2)}, u32[]{:S(2)}) collective-permute-start(bf16[80,14]{0,1:T(8,128)(2,1)S(1)} %pad_maximum_fusion.4), channel_id=1, source_target_pairs={{0,1},{1,2},{2,3},{4,5},{5,6},{6,7},{8,9},{9,10},{10,11},{12,13},{... | collective-permute-start | bytes 6728 | tf_op jit(solution)/shard_map/ppermute | solution.py:37
  10.2 23.1 %collective-permute-start.1 = (bf16[80,640]{1,0:T(8,128)(2,1)S(1)}, bf16[80,640]{1,0:T(8,128)(2,1)S(1)}, u32[]{:S(2)}, u32[]{:S(2)}) collective-permute-start(bf16[80,640]{1,0:T(8,128)(2,1)S(1)} %pad_maximum_fusion.2), channel_id=1, source_target_pairs={{0,4},{4,8},{8,12},{1,5},{5,9},{9,13},{2,6},{6,10},{10,14},{3,7},{... | collective-permute-start | bytes 307208 | tf_op jit(solution)/shard_map/ppermute | solution.py:35
  13.5 19.8 %collective-permute-start = (bf16[80,640]{1,0:T(8,128)(2,1)S(1)}, bf16[80,640]{1,0:T(8,128)(2,1)S(1)}, u32[]{:S(2)}, u32[]{:S(2)}) collective-permute-start(bf16[80,640]{1,0:T(8,128)(2,1)S(1)} %pad_maximum_fusion.1), channel_id=1, source_target_pairs={{4,0},{8,4},{12,8},{5,1},{9,5},{13,9},{6,2},{10,6},{14,10},{7,3},{... | collective-permute-start | bytes 307208 | tf_op jit(solution)/shard_map/ppermute | solution.py:36
  15.4 17.8 %all-to-all-start = ((s32[4,256,1]{1,2,0:T(1,128)}), s32[4,256,1]{1,2,0:T(1,128)S(1)}, u32[]{:S(2)}, u32[]{:S(2)}) async-start(s32[4,256,1]{1,2,0:T(1,128)} %compare_select_fusion.1), calls=%async_computation | async-start | bytes 8192 | tf_op jit(solution)/shard_map/all_to_all | solution.py:132
  23.8 1.3 %copy-start.1 = (s32[24]{0:T(128)S(1)}, s32[24]{0:T(128)}, u32[]{:S(2)}) copy-start(s32[24]{0:T(128)} %param.19) | copy-start | bytes 292
  32.2 1.8 %copy-start.28 = (f32[80]{0:T(128)S(1)}, f32[80]{0:T(128)}, u32[]{:S(2)}) copy-start(f32[80]{0:T(128)} %param.12) | copy-start | bytes 964
  33.3 0.6 copy-start.20
  33.3 0.6 copy-start.22
  36.7 3.2 %copy-start.2 = (f32[80,2048]{1,0:T(8,128)}, f32[80,2048]{1,0:T(8,128)S(1)}, u32[]{:S(2)}) copy-start(f32[80,2048]{1,0:T(8,128)S(1)} %convolution_bitcast_fusion.2) | copy-start | bytes 1966084
  40.1 5.2 %copy-start.21 = (bf16[80,640]{1,0:T(8,128)(2,1)S(1)}, bf16[80,640]{1,0:T(8,128)(2,1)}, u32[]{:S(2)}) copy-start(bf16[80,640]{1,0:T(8,128)(2,1)} %copy-done.20) | copy-start | bytes 307204
  40.1 5.9 %copy-start.23 = (bf16[80,640]{1,0:T(8,128)(2,1)S(1)}, bf16[80,640]{1,0:T(8,128)(2,1)}, u32[]{:S(2)}) copy-start(bf16[80,640]{1,0:T(8,128)(2,1)} %copy-done.22) | copy-start | bytes 307204
  40.3 6.5 %collective-permute-start.4 = (f32[80,256]{1,0:T(8,128)S(1)}, f32[80,256]{1,0:T(8,128)S(1)}, u32[]{:S(2)}, u32[]{:S(2)}) collective-permute-start(f32[80,256]{1,0:T(8,128)S(1)} %bitcast.157), channel_id=1, source_target_pairs={{0,4},{4,8},{8,12},{12,0},{1,5},{5,9},{9,13},{13,1},{2,6},{6,10},{... | collective-permute-start | bytes 245768 | tf_op jit(solution)/shard_map/ppermute | solution.py:140
  41.9 8.1 %collective-permute-start.5 = (f32[80,256]{1,0:T(8,128)S(1)}, f32[80,256]{1,0:T(8,128)S(1)}, u32[]{:S(2)}, u32[]{:S(2)}) collective-permute-start(f32[80,256]{1,0:T(8,128)S(1)} %bitcast.158), channel_id=1, source_target_pairs={{0,8},{4,12},{8,0},{12,4},{1,9},{5,13},{9,1},{13,5},{2,10},{6,14},... | collective-permute-start | bytes 245768 | tf_op jit(solution)/shard_map/ppermute | solution.py:140
  44.1 5.9 %collective-permute-start.6 = (f32[80,256]{1,0:T(8,128)S(1)}, f32[80,256]{1,0:T(8,128)S(1)}, u32[]{:S(2)}, u32[]{:S(2)}) collective-permute-start(f32[80,256]{1,0:T(8,128)S(1)} %bitcast.159), channel_id=1, source_target_pairs={{0,12},{4,0},{8,4},{12,8},{1,13},{5,1},{9,5},{13,9},{2,14},{6,2},{... | collective-permute-start | bytes 245768 | tf_op jit(solution)/shard_map/ppermute | solution.py:140
  46.0 4.7 %copy-start.4 = (pred[256,2304]{1,0:T(32,128)(4,1)S(1)}, pred[256,2304]{1,0:T(32,128)(4,1)}, u32[]{:S(2)}) copy-start(pred[256,2304]{1,0:T(32,128)(4,1)} %fusion.6) | copy-start | bytes 1769476
  50.1 1.5 %copy-start.8 = (f32[10,8,6,384]{3,1,2,0:T(8,128)S(1)}, f32[10,8,6,384]{3,1,2,0:T(8,128)}, u32[]{:S(2)}) copy-start(f32[10,8,6,384]{3,1,2,0:T(8,128)} %copy.135) | copy-start | bytes 2211844
  50.7 1.2 %copy-start.6 = (f32[80,2303]{1,0:T(8,128)S(1)}, f32[80,2303]{1,0:T(8,128)}, u32[]{:S(2)}) copy-start(f32[80,2303]{1,0:T(8,128)} %get-tuple-element.21) | copy-start | bytes 2210884
  50.7 1.4 %copy-start.7 = (f32[80,2303]{1,0:T(8,128)S(1)}, f32[80,2303]{1,0:T(8,128)}, u32[]{:S(2)}) copy-start(f32[80,2303]{1,0:T(8,128)} %get-tuple-element.22) | copy-start | bytes 2210884
  50.7 1.4 %copy-start.18 = (f32[80,384]{1,0:T(8,128)S(1)}, f32[80,384]{1,0:T(8,128)}, u32[]{:S(2)}) copy-start(f32[80,384]{1,0:T(8,128)} %slice_convert_fusion) | copy-start | bytes 368644
  50.7 1.4 %copy-start.19 = (f32[80,384]{1,0:T(8,128)S(1)}, f32[80,384]{1,0:T(8,128)}, u32[]{:S(2)}) copy-start(f32[80,384]{1,0:T(8,128)} %slice_convert_fusion.1) | copy-start | bytes 368644
  50.7 1.4 %copy-start.24 = (f32[80]{0:T(128)S(1)}, f32[80]{0:T(128)}, u32[]{:S(2)}) copy-start(f32[80]{0:T(128)} %param.14) | copy-start | bytes 964
  50.7 1.4 %copy-start.25 = (f32[80]{0:T(128)S(1)}, f32[80]{0:T(128)}, u32[]{:S(2)}) copy-start(f32[80]{0:T(128)} %param.13) | copy-start | bytes 964
  55.8 14.1 %collective-permute-start.9 = (bf16[80,6]{0,1:T(8,128)(2,1)S(1)}, bf16[80,6]{0,1:T(8,128)(2,1)S(1)}, u32[]{:S(2)}, u32[]{:S(2)}) collective-permute-start(bf16[80,6]{0,1:T(8,128)(2,1)S(1)} %bitcast.175), channel_id=1, source_target_pairs={{1,0},{2,1},{3,2},{5,4},{6,5},{7,6},{9,8},{10,9},{11,10},{13,12},{... | collective-permute-start | bytes 2888 | tf_op jit(solution)/shard_map/ppermute | solution.py:38
  58.7 12.4 %collective-permute-start.10 = (bf16[80,6]{0,1:T(8,128)(2,1)S(1)}, bf16[80,6]{0,1:T(8,128)(2,1)S(1)}, u32[]{:S(2)}, u32[]{:S(2)}) collective-permute-start(bf16[80,6]{0,1:T(8,128)(2,1)S(1)} %bitcast.173), channel_id=1, source_target_pairs={{0,1},{1,2},{2,3},{4,5},{5,6},{6,7},{8,9},{9,10},{10,11},{12,13},{... | collective-permute-start | bytes 2888 | tf_op jit(solution)/shard_map/ppermute | solution.py:37
  62.7 8.9 %collective-permute-start.7 = (bf16[80,384]{1,0:T(8,128)(2,1)S(1)}, bf16[80,384]{1,0:T(8,128)(2,1)S(1)}, u32[]{:S(2)}, u32[]{:S(2)}) collective-permute-start(bf16[80,384]{1,0:T(8,128)(2,1)S(1)} %bitcast.160), channel_id=1, source_target_pairs={{4,0},{8,4},{12,8},{5,1},{9,5},{13,9},{6,2},{10,6},{14,10},{7,3},{... | collective-permute-start | bytes 184328 | tf_op jit(solution)/shard_map/ppermute | solution.py:36
  64.0 7.6 %collective-permute-start.8 = (bf16[80,384]{1,0:T(8,128)(2,1)S(1)}, bf16[80,384]{1,0:T(8,128)(2,1)S(1)}, u32[]{:S(2)}, u32[]{:S(2)}) collective-permute-start(bf16[80,384]{1,0:T(8,128)(2,1)S(1)} %bitcast.162), channel_id=1, source_target_pairs={{0,4},{4,8},{8,12},{1,5},{5,9},{9,13},{2,6},{6,10},{10,14},{3,7},{... | collective-permute-start | bytes 184328 | tf_op jit(solution)/shard_map/ppermute | solution.py:35
  71.2 1.1 copy-start.15
  71.4 1.2 %copy-start.9 = (f32[80,2303]{1,0:T(8,128)S(1)}, f32[80,2303]{1,0:T(8,128)}, u32[]{:S(2)}) copy-start(f32[80,2303]{1,0:T(8,128)} %get-tuple-element.18) | copy-start | bytes 2210884
  71.4 1.4 %copy-start.11 = (f32[10,8,6,384]{3,1,2,0:T(8,128)S(1)}, f32[10,8,6,384]{3,1,2,0:T(8,128)}, u32[]{:S(2)}) copy-start(f32[10,8,6,384]{3,1,2,0:T(8,128)} %copy.137) | copy-start | bytes 2211844
  71.4 1.6 %copy-start.14 = (f32[80,1920]{1,0:T(8,128)S(1)}, f32[80,1920]{1,0:T(8,128)}, u32[]{:S(2)}) copy-start(f32[80,1920]{1,0:T(8,128)} %get-tuple-element.19) | copy-start | bytes 1843204
  75.2 12.4 %collective-permute-start.13 = (bf16[80,6]{0,1:T(8,128)(2,1)S(1)}, bf16[80,6]{0,1:T(8,128)(2,1)S(1)}, u32[]{:S(2)}, u32[]{:S(2)}) collective-permute-start(bf16[80,6]{0,1:T(8,128)(2,1)S(1)} %bitcast.176), channel_id=1, source_target_pairs={{1,0},{2,1},{3,2},{5,4},{6,5},{7,6},{9,8},{10,9},{11,10},{13,12},{... | collective-permute-start | bytes 2888 | tf_op jit(solution)/shard_map/ppermute | solution.py:38
  77.3 11.7 %collective-permute-start.14 = (bf16[80,6]{0,1:T(8,128)(2,1)S(1)}, bf16[80,6]{0,1:T(8,128)(2,1)S(1)}, u32[]{:S(2)}, u32[]{:S(2)}) collective-permute-start(bf16[80,6]{0,1:T(8,128)(2,1)S(1)} %bitcast.174), channel_id=1, source_target_pairs={{0,1},{1,2},{2,3},{4,5},{5,6},{6,7},{8,9},{9,10},{10,11},{12,13},{... | collective-permute-start | bytes 2888 | tf_op jit(solution)/shard_map/ppermute | solution.py:37
  81.2 8.2 %collective-permute-start.11 = (bf16[80,384]{1,0:T(8,128)(2,1)S(1)}, bf16[80,384]{1,0:T(8,128)(2,1)S(1)}, u32[]{:S(2)}, u32[]{:S(2)}) collective-permute-start(bf16[80,384]{1,0:T(8,128)(2,1)S(1)} %bitcast.161), channel_id=1, source_target_pairs={{4,0},{8,4},{12,8},{5,1},{9,5},{13,9},{6,2},{10,6},{14,10},{7,3},{... | collective-permute-start | bytes 184328 | tf_op jit(solution)/shard_map/ppermute | solution.py:36
  82.5 6.9 %collective-permute-start.12 = (bf16[80,384]{1,0:T(8,128)(2,1)S(1)}, bf16[80,384]{1,0:T(8,128)(2,1)S(1)}, u32[]{:S(2)}, u32[]{:S(2)}) collective-permute-start(bf16[80,384]{1,0:T(8,128)(2,1)S(1)} %bitcast.163), channel_id=1, source_target_pairs={{0,4},{4,8},{8,12},{1,5},{5,9},{9,13},{2,6},{6,10},{10,14},{3,7},{... | collective-permute-start | bytes 184328 | tf_op jit(solution)/shard_map/ppermute | solution.py:35
  89.2 1.1 copy-start.10
  89.2 1.3 %copy-start.12 = (f32[80,1920]{1,0:T(8,128)S(1)}, f32[80,1920]{1,0:T(8,128)}, u32[]{:S(2)}) copy-start(f32[80,1920]{1,0:T(8,128)} %get-tuple-element.15) | copy-start | bytes 1843204
  89.2 1.5 %copy-start.13 = (f32[80,1920]{1,0:T(8,128)S(1)}, f32[80,1920]{1,0:T(8,128)}, u32[]{:S(2)}) copy-start(f32[80,1920]{1,0:T(8,128)} %get-tuple-element.16) | copy-start | bytes 1843204
  90.7 1.3 %copy-start.5 = (pred[256,2304]{1,0:T(32,128)(4,1)S(1)}, pred[256,2304]{1,0:T(32,128)(4,1)}, u32[]{:S(2)}) copy-start(pred[256,2304]{1,0:T(32,128)(4,1)} %fusion.6) | copy-start | bytes 1769476
  94.0 13.8 %all-to-all-start.1 = ((f32[80,4,256]{2,0,1:T(8,128)}), f32[80,4,256]{2,0,1:T(8,128)S(1)}, u32[]{:S(2)}, u32[]{:S(2)}) async-start(f32[80,4,256]{2,0,1:T(8,128)} %broadcast_select_fusion.1), calls=%async_computation.1 | async-start | bytes 655360 | tf_op jit(solution)/shard_map/all_to_all | solution.py:183
  114.4 1.1 copy-start.3
  114.4 1.1 copy-start.29
